TPU v7x, 256 devices: a whole 4x4x8 slice. The times are simulated.
256 devices in a mesh: dp: 32 (over y, x, core), tensor: 8 (over z).
Axes of the slice: x: 4, y: 4, z: 8, core: 2. Of those that a mesh axis runs over, the one named last changes fastest.
Arguments:
- tokens: bfloat16 [8192, 8192], P('dp'), may hold values from -6 to 6
- router_weight: bfloat16 [8192, 32], replicated, may hold values from -0.0625 to 0.0625
- gate_weight: bfloat16 [14336, 8192], P(('dp', 'tensor')), may hold values from -0.0625 to 0.0625
- up_weight: bfloat16 [14336, 8192], P(('dp', 'tensor')), may hold values from -0.0625 to 0.0625
- down_weight: bfloat16 [14336, 8192], P(('dp', 'tensor')), may hold values from -0.25 to 0.25
- cluster_of: int32 [14336, 1], P('dp'), may hold values from 0 to 31; in each aligned block of 448 rows (0 to 447, 448 to 895, ...) at most 28 rows name the same one
- expert_ids: int32 [8192, 2], P('dp'), may hold values from 0 to 31, all different within a row; in each aligned block of 256 rows (0 to 255, 256 to 511, ...) at most 32 rows name the same one
Outputs:
- mixed_out: bfloat16 [8192, 8192], P('dp', 'tensor')
Inputs may be any that keep to these rules, and one draw needn't show every extreme that they name: `expert_ids`: in each aligned block of 256 rows (the tokens of one dp index) no expert is named by more than 32 rows, a bound that some block reaches; a row names two different experts; every expert is named somewhere. `cluster_of`: in each aligned block of 448 hidden units no cluster holds more than 28 units, and some cluster holds exactly 28; every cluster holds some unit.
All inputs are finite; a program needn't handle non-finite values.
Results may differ from a plain program's by a relative error of at most 0.023.
Values may be sent and summed in bfloat16 or wider, within the bound.
No kernel may reach another device: no remote copies, remote signals or barrier semaphores. Data moves between devices by JAX's collectives and lax.ppermute only.
A program may use at most 64 MiB of HBM per device.

v0:
```python
import jax
import jax.numpy as jnp
from jax import lax
from jax.sharding import PartitionSpec as P


def place_rows(labels, bin_count, capacity):
    count_rows = labels.shape[0]
    onehot = (labels[:, None] == jnp.arange(bin_count, dtype=jnp.int32)[None, :]).astype(jnp.int32)
    before = jnp.cumsum(onehot, axis=0) - onehot
    rank_in = jnp.sum(before * onehot, axis=1)
    position = labels * capacity + rank_in
    slot_list = jnp.full((bin_count * capacity,), count_rows, jnp.int32)
    slot_list = slot_list.at[position].set(jnp.arange(count_rows, dtype=jnp.int32))
    return (slot_list, position)


def with_zero_row(matrix):
    pad = jnp.zeros((1,) + matrix.shape[1:], matrix.dtype)
    return jnp.concatenate([matrix, pad], axis=0)


def against(left_side, right_side):
    return lax.dot_general(
        left_side, right_side, (((1,), (1,)), ((), ())), preferred_element_type=jnp.float32
    )


def on_device(tokens, router_weight, gate_weight, up_weight, down_weight, cluster_of, expert_ids):
    owners = lax.axis_size("dp")
    tensor_count = lax.axis_size("tensor")
    width_part = tokens.shape[1] // tensor_count
    token_count = tokens.shape[0]
    logits = jnp.dot(tokens, router_weight, preferred_element_type=jnp.float32)
    scores = jax.nn.sigmoid(jnp.take_along_axis(logits, expert_ids, axis=1))
    mixing = scores / jnp.sum(scores, axis=1, keepdims=True)
    stacked = jnp.stack([gate_weight, up_weight, down_weight], axis=1)
    rows = lax.all_to_all(stacked, "tensor", split_axis=2, concat_axis=0, tiled=True)
    unit_cap = 2 * rows.shape[0] // owners
    unit_list, unit_spot = place_rows(cluster_of[:, 0], owners, unit_cap)
    pick = with_zero_row(rows)[unit_list]
    own = lax.all_to_all(pick, "dp", split_axis=0, concat_axis=0, tiled=True)
    capacity = 4 * token_count // owners
    flat_ids = expert_ids.reshape(-1)
    slot_list, slot_spot = place_rows(flat_ids, owners, capacity)
    features = lax.dynamic_slice_in_dim(
        tokens, lax.axis_index("tensor") * width_part, width_part, 1
    )
    outgoing = with_zero_row(features)[slot_list // 2]
    arrived = lax.all_to_all(outgoing, "dp", split_axis=0, concat_axis=0, tiled=True)
    gate_part = against(arrived, own[:, 0, :]).astype(jnp.bfloat16)
    up_part = against(arrived, own[:, 1, :]).astype(jnp.bfloat16)
    both = jnp.stack([gate_part, up_part], axis=1)
    summed = lax.psum_scatter(both, "tensor", scatter_dimension=0, tiled=True).astype(jnp.float32)
    hidden_part = (jax.nn.silu(summed[:, 0, :]) * summed[:, 1, :]).astype(jnp.bfloat16)
    hidden = lax.all_gather(hidden_part, "tensor", axis=0, tiled=True)
    expert_out = jnp.dot(hidden, own[:, 2, :], preferred_element_type=jnp.float32).astype(
        jnp.bfloat16
    )
    returned = lax.all_to_all(expert_out, "dp", split_axis=0, concat_axis=0, tiled=True)
    picked_out = returned[slot_spot].reshape(token_count, 2, width_part)
    mixed_out = jnp.sum(mixing[:, :, None] * picked_out.astype(jnp.float32), axis=1)
    return mixed_out.astype(jnp.bfloat16)


def solution(mesh):
    in_specs = (
        P("dp", None),
        P(),
        P(("dp", "tensor"), None),
        P(("dp", "tensor"), None),
        P(("dp", "tensor"), None),
        P("dp", None),
        P("dp", None),
    )
    out_specs = P("dp", "tensor")
    return jax.shard_map(
        on_device, mesh=mesh, in_specs=in_specs, out_specs=out_specs, check_vma=False
    )
```

profile of v0, /device:TPU:1, one launch (start us, length us, event | category | flops | bytes accessed | tf_op | source)
XLA Modules:
  0.0 451.2 jit_solution(5226104023529939072)
XLA Ops:
  6.5 2.1 pad_maximum_fusion.1
  8.6 8.4 %copy.72 = bf16[56,3,8192]{0,1,2:T(4,128)(2,1)} copy(bf16[56,3,8192]{2,0,1:T(8,128)(2,1)S(1)} %pad_maximum_fusion.1) | data formatting | bytes 5505024 | tf_op jit(solution)/shard_map/stack | solution.py:37
  17.0 12.4 %reshape.154 = bf16[8,2,86016]{2,1,0:T(2,128)(2,1)} reshape(bf16[8192,3,56]{2,1,0:T(4,128)(2,1)} %bitcast.87) | data formatting | bytes 5505024
  29.4 9.1 %all-to-all-start.1 = ((bf16[8,2,86016]{2,1,0:T(2,128)(2,1)}), bf16[8,2,86016]{2,1,0:T(2,128)(2,1)S(1)}, u32[]{:S(2)}, u32[]{:S(2)}) async-start(bf16[8,2,86016]{2,1,0:T(2,128)(2,1)} %reshape.154), calls=%async_computation.1 | async-start | bytes 5505024 | tf_op jit(solution)/shard_map/all_to_all | solution.py:38
  38.6 1.2 reduce-window.16
  39.7 0.2 slice_reduce_fusion
  40.2 2.9 scatter_custom_fusion.1
  43.1 61.2 %all-to-all-done.1 = bf16[8,2,86016]{2,1,0:T(2,128)(2,1)S(1)} async-done(((bf16[8,2,86016]{2,1,0:T(2,128)(2,1)}), bf16[8,2,86016]{2,1,0:T(2,128)(2,1)S(1)}, u32[]{:S(2)}, u32[]{:S(2)}) %all-to-all-start.1) | async-done | bytes 2752544 | tf_op jit(solution)/shard_map/all_to_all | solution.py:38
  104.3 13.2 %reshape.155 = bf16[8192,3,56]{2,1,0:T(4,128)(2,1)} reshape(bf16[8,2,86016]{2,1,0:T(2,128)(2,1)S(1)} %all-to-all-done.1) | data formatting | bytes 5505024
  117.5 10.6 %copy.79 = bf16[56,3,8,1024]{3,0,2,1:T(8,128)(2,1)S(1)} copy(bf16[56,3,8,1024]{0,1,3,2:T(4,128)(2,1)} %bitcast.88) | data formatting | bytes 5505024 | tf_op jit(solution)/shard_map/all_to_all | solution.py:38
  128.1 2.4 copy.75
  130.5 3.2 concatenate.7
  133.7 33.1 %gather_fusion.1 = bf16[896,3,1024]{2,1,0:T(4,128)(2,1)} fusion(bf16[449,3,1024]{2,1,0:T(4,128)(2,1)} %concatenate.7, s32[1024]{0:T(1024)S(1)} %pad_clamp_fusion.1), kind=kCustom, calls=%fused_computation.1 | custom fusion | bytes 11013632 | tf_op jit(solution)/shard_map/gather | solution.py:41
  166.8 7.6 %all-to-all-start.2 = ((bf16[896,3,1024]{2,1,0:T(4,128)(2,1)}), bf16[896,3,1024]{2,1,0:T(4,128)(2,1)}, u32[]{:S(2)}, u32[]{:S(2)}) async-start(bf16[896,3,1024]{2,1,0:T(4,128)(2,1)} %gather_fusion.1), calls=%async_computation.2 | async-start | bytes 14680064 | tf_op jit(solution)/shard_map/all_to_all | solution.py:42
  174.4 0.1 copy.69
  174.6 0.1 eq.51
  174.7 0.1 eq.47
  174.9 1.1 constant_dynamic-slice_fusion
  176.0 1.2 reduce-window.14
  177.2 0.2 slice_reduce_fusion.1
  177.5 0.1 copy.68
  177.6 0.1 mul.48
  177.8 0.1 fusion.16
  177.9 2.4 scatter_custom_fusion
  180.4 5.4 %gather_fusion = bf16[1024,1024]{1,0:T(8,128)(2,1)} fusion(bf16[257,1024]{1,0:T(8,128)(2,1)S(1)} %concatenate.6, s32[1024]{0:T(1024)S(1)} %fusion.21), kind=kCustom, calls=%fused_computation | custom fusion | bytes 4198400 | tf_op jit(solution)/shard_map/gather | solution.py:49
  185.7 75.9 %all-to-all-done.2 = bf16[896,3,1024]{2,1,0:T(4,128)(2,1)} async-done(((bf16[896,3,1024]{2,1,0:T(4,128)(2,1)}), bf16[896,3,1024]{2,1,0:T(4,128)(2,1)}, u32[]{:S(2)}, u32[]{:S(2)}) %all-to-all-start.2) | async-done | bytes 5505056 | tf_op jit(solution)/shard_map/all_to_all | solution.py:42
  261.6 8.7 %all-to-all-start = ((bf16[32,32,1024]{2,1,0:T(8,128)(2,1)}), bf16[32,32,1024]{2,1,0:T(8,128)(2,1)S(1)}, u32[]{:S(2)}, u32[]{:S(2)}) async-start(bf16[32,32,1024]{2,1,0:T(8,128)(2,1)} %bitcast.4), calls=%async_computation | async-start | bytes 4194304 | tf_op jit(solution)/shard_map/all_to_all | solution.py:50
  270.4 18.2 %fusion.28 = (bf16[896,1,1024]{2,1,0:T(2,128)(2,1)}, bf16[896,1,1024]{2,1,0:T(2,128)(2,1)}, bf16[896,1,1024]{2,1,0:T(2,128)(2,1)}) fusion(bf16[896,3,1024]{2,1,0:T(4,128)(2,1)} %all-to-all-done.2), kind=kLoop, calls=%fused_computation.70 | loop fusion | bytes 11010048 | tf_op jit(solution)/shard_map/slice | solution.py:57
  288.6 10.0 %all-to-all-done = bf16[32,32,1024]{2,1,0:T(8,128)(2,1)S(1)} async-done(((bf16[32,32,1024]{2,1,0:T(8,128)(2,1)}), bf16[32,32,1024]{2,1,0:T(8,128)(2,1)S(1)}, u32[]{:S(2)}, u32[]{:S(2)}) %all-to-all-start) | async-done | bytes 2097184 | tf_op jit(solution)/shard_map/all_to_all | solution.py:50
  298.6 4.6 %convert_bitcast_fusion.1 = bf16[1024,1,896]{2,0,1:T(8,128)(2,1)S(1)} fusion(bf16[1024,1024]{1,0:T(8,128)(2,1)S(1)} %bitcast.91, bf16[896,1,1024]{2,1,0:T(2,128)(2,1)} %get-tuple-element.9), kind=kOutput, calls=%fused_computation.19 | convolution fusion | flops 1879965696 | bytes 5767168 | tf_op jit(solution)/shard_map/dot_general | solution.py:24
  303.2 2.4 convert_bitcast_fusion
  305.6 2.2 pad_maximum_fusion
  307.9 44.0 %reduce-scatter.2.cloned.1.call-done = bf16[128,2,896]{2,0,1:T(8,128)(2,1)} async-done(((bf16[1024,2,896]{2,0,1:T(8,128)(2,1)}), bf16[128,2,896]{2,0,1:T(8,128)(2,1)}) %reduce-scatter.2.cloned.1.call-update) | async-done | bytes 458768 | tf_op jit(solution)/shard_map/reduce_scatter | solution.py:54
  351.9 1.1 convert_element_type.40
  353.0 0.8 fusion.13
  353.8 35.5 %all-gather.2.cloned.1.call-done = bf16[1024,896]{1,0:T(8,128)(2,1)} async-done(((bf16[128,896]{1,0:T(8,128)(2,1)}), bf16[1024,896]{1,0:T(8,128)(2,1)}) %all-gather.2.cloned.1.call-update) | async-done | bytes 1835024 | tf_op jit(solution)/shard_map/all_gather | solution.py:56
  389.3 6.3 %convolution_convert_fusion = bf16[1024,1024]{1,0:T(8,128)(2,1)} fusion(bf16[1024,896]{1,0:T(8,128)(2,1)} %all-gather.2.cloned.1.call-done, bf16[896,1,1024]{2,1,0:T(2,128)(2,1)} %get-tuple-element.7), kind=kOutput, calls=%fused_computation.9 | convolution fusion | flops 1880096768 | bytes 5767168 | tf_op jit(solution)/shard_map/dot_general | solution.py:57
  395.6 11.6 %all-to-all-start.3 = ((bf16[32,32,1024]{2,1,0:T(8,128)(2,1)}), bf16[32,32,1024]{2,1,0:T(8,128)(2,1)S(1)}, u32[]{:S(2)}, u32[]{:S(2)}) async-start(bf16[32,32,1024]{2,1,0:T(8,128)(2,1)} %bitcast.90), calls=%async_computation.4 | async-start | bytes 4194304 | tf_op jit(solution)/shard_map/all_to_all | solution.py:60
  407.2 0.1 copy.65
  407.4 0.1 reshape.119
  407.5 3.5 fusion.29
  411.1 4.5 %gather_fusion.3 = f32[512]{0:T(512)S(1)} fusion(f32[256,32]{0,1:T(8,128)S(1)} %fusion.29, s32[512]{0:T(512)S(1)} %reshape.119), kind=kCustom, calls=%fused_computation.3 | custom fusion | bytes 8192 | tf_op jit(solution)/shard_map/jit(take_along_axis)/gather | solution.py:35
  415.7 0.1 reshape.122
  415.9 0.1 copy.67
  416.1 19.6 %all-to-all-done.3 = bf16[32,32,1024]{2,1,0:T(8,128)(2,1)S(1)} async-done(((bf16[32,32,1024]{2,1,0:T(8,128)(2,1)}), bf16[32,32,1024]{2,1,0:T(8,128)(2,1)S(1)}, u32[]{:S(2)}, u32[]{:S(2)}) %all-to-all-start.3) | async-done | bytes 2097184 | tf_op jit(solution)/shard_map/all_to_all | solution.py:60
  435.7 2.8 gather_fusion.2
  438.5 2.4 reshape.94
  440.9 3.5 multiply_reduce_fusion
  (37 shorter events, 0.6 us)
Async XLA Ops:
  6.5 401.0 %copy-start = (bf16[8192,32]{0,1:T(8,128)(2,1)S(1)}, bf16[8192,32]{0,1:T(8,128)(2,1)}, u32[]{:S(2)}) copy-start(bf16[8192,32]{0,1:T(8,128)(2,1)} %param.8) | copy-start | bytes 1572868
  29.4 9.1 %copy-start.4 = (s32[448,1]{0,1:T(1,128)S(1)}, s32[448,1]{0,1:T(1,128)}, u32[]{:S(2)}) copy-start(s32[448,1]{0,1:T(1,128)} %param.12) | copy-start | bytes 5380
  29.4 74.9 %all-to-all-start.1 = ((bf16[8,2,86016]{2,1,0:T(2,128)(2,1)}), bf16[8,2,86016]{2,1,0:T(2,128)(2,1)S(1)}, u32[]{:S(2)}, u32[]{:S(2)}) async-start(bf16[8,2,86016]{2,1,0:T(2,128)(2,1)} %reshape.154), calls=%async_computation.1 | async-start | bytes 5505024 | tf_op jit(solution)/shard_map/all_to_all | solution.py:38
  166.8 7.7 %copy-start.3 = (s32[256,2]{0,1:T(2,128)S(1)}, s32[256,2]{0,1:T(2,128)}, u32[]{:S(2)}) copy-start(s32[256,2]{0,1:T(2,128)} %param.13) | copy-start | bytes 6148
  166.8 94.8 %all-to-all-start.2 = ((bf16[896,3,1024]{2,1,0:T(4,128)(2,1)}), bf16[896,3,1024]{2,1,0:T(4,128)(2,1)}, u32[]{:S(2)}, u32[]{:S(2)}) async-start(bf16[896,3,1024]{2,1,0:T(4,128)(2,1)} %gather_fusion.1), calls=%async_computation.2 | async-start | bytes 14680064 | tf_op jit(solution)/shard_map/all_to_all | solution.py:42
  261.6 37.0 %all-to-all-start = ((bf16[32,32,1024]{2,1,0:T(8,128)(2,1)}), bf16[32,32,1024]{2,1,0:T(8,128)(2,1)S(1)}, u32[]{:S(2)}, u32[]{:S(2)}) async-start(bf16[32,32,1024]{2,1,0:T(8,128)(2,1)} %bitcast.4), calls=%async_computation | async-start | bytes 4194304 | tf_op jit(solution)/shard_map/all_to_all | solution.py:50
  270.3 81.6 %reduce-scatter.2.cloned.1.call-start = ((), (), s32[]{:S(2)}) async-start(), calls=%async_computation.5 | async-start | bytes 4128768 | tf_op jit(solution)/shard_map/reduce_scatter | solution.py:54
  298.6 4.6 %copy-start.2 = (bf16[896,1,1024]{2,1,0:T(2,128)(2,1)S(1)}, bf16[896,1,1024]{2,1,0:T(2,128)(2,1)}, u32[]{:S(2)}) copy-start(bf16[896,1,1024]{2,1,0:T(2,128)(2,1)} %get-tuple-element.8) | copy-start | bytes 5505028
  307.8 81.5 %all-gather.2.cloned.1.call-start = ((), (), s32[]{:S(2)}) async-start(), calls=%async_computation.6 | async-start | bytes 2064384 | tf_op jit(solution)/shard_map/all_gather | solution.py:56
  395.6 40.1 %all-to-all-start.3 = ((bf16[32,32,1024]{2,1,0:T(8,128)(2,1)}), bf16[32,32,1024]{2,1,0:T(8,128)(2,1)S(1)}, u32[]{:S(2)}, u32[]{:S(2)}) async-start(bf16[32,32,1024]{2,1,0:T(8,128)(2,1)} %bitcast.90), calls=%async_computation.4 | async-start | bytes 4194304 | tf_op jit(solution)/shard_map/all_to_all | solution.py:60
  435.7 8.6 %copy-start.1 = (bf16[8192,32]{0,1:T(8,128)(2,1)S(1)}, bf16[8192,32]{0,1:T(8,128)(2,1)}, u32[]{:S(2)}) copy-start(bf16[8192,32]{0,1:T(8,128)(2,1)} %param.8) | copy-start | bytes 1572868
Sparse Core Ops, SparseCore 0:
  307.9 43.9 reduce-scatter.1
  353.9 35.3 all-gather.1
where the time goes:
time: 452 us; the launch traced here: 451 us
  waiting for transfers between devices  246 us (54%)
  local copies, waits for them, and re-layouts  125 us (28%)
  starting transfers between devices  37.2 us (8%)
  matrix products  16.8 us (4%)
  between operations  13.8 us (3%)
  other arithmetic  12.4 us (3%)
    all_to_all x1, waiting for transfers between devices, on_device(): own = lax.all_to_all(pick, 'dp', split_axis=0, concat_axis=0, tiled=True)  75.9 us
    all_to_all x1, waiting for transfers between devices, on_device(): lax.all_to_all(stacked, 'tensor', split_axis=2, concat_axis=0, tiled=True)  61.2 us
    reduce_scatter x1, waiting for transfers between devices, on_device(): lax.psum_scatter(both, 'tensor', scatter_dimension=0, tiled=True)  44 us
    all_gather x1, waiting for transfers between devices, on_device(): hidden = lax.all_gather(hidden_part, 'tensor', axis=0, tiled=True)  35.5 us
    gather x1, local copies, waits for them, and re-layouts, on_device(): pick = with_zero_row(rows)[unit_list]  33.1 us
    unnamed x13, local copies, waits for them, and re-layouts  25.7 us
    all_to_all x1, waiting for transfers between devices, on_device(): lax.all_to_all(expert_out, 'dp', split_axis=0, concat_axis=0, tiled=True)  19.6 us
    slice x1, local copies, waits for them, and re-layouts, on_device(): own[:, 2, :]  18.2 us
  transfers between devices with their start and end apart: 6, of which 6 were waited for; matrix products, arithmetic and copies ran while one was open for 9% of the time, Pallas kernels for 0%

commit v1 on v0

--- a/solution.py
+++ b/solution.py
@@ -2,6 +2,13 @@
 import jax.numpy as jnp
 from jax import lax
 from jax.sharding import PartitionSpec as P
+
+
+def review_stocks(block_here, chip_axis):
+    pieces_in = []
+    for _ in range(lax.axis_size(chip_axis)):
+        pieces_in.append(block_here)
+    return jnp.concatenate(lax.all_to_all(jnp.stack(pieces_in, 0), chip_axis, 0, 0), 0)
 
 
 def place_rows(labels, bin_count, capacity):
@@ -53,7 +60,7 @@
     both = jnp.stack([gate_part, up_part], axis=1)
     summed = lax.psum_scatter(both, "tensor", scatter_dimension=0, tiled=True).astype(jnp.float32)
     hidden_part = (jax.nn.silu(summed[:, 0, :]) * summed[:, 1, :]).astype(jnp.bfloat16)
-    hidden = lax.all_gather(hidden_part, "tensor", axis=0, tiled=True)
+    hidden = review_stocks(hidden_part, "tensor")
     expert_out = jnp.dot(hidden, own[:, 2, :], preferred_element_type=jnp.float32).astype(
         jnp.bfloat16
     )

time: 452 us -> 468 us (1.035); the launches traced: 451 us -> 460 us
  blocking collectives: 0 us -> 48.1 us
  waiting for transfers between devices: 246 us -> 211 us
    all_to_all x0 -> x1, blocking collectives: none -> 48.1 us  [review_stocks(): lax.all_to_all(jnp.stack(pieces_in, 0), chip_axis, 0, 0)]
    all_gather x1 -> x0, waiting for transfers between devices: 35.5 us -> none  [on_device(): hidden = lax.all_gather(hidden_part, 'tensor', axis=0, tiled=True)]
  transfers between devices with their start and end apart: 6 -> 5, of which waited for: 6 -> 5; matrix products, arithmetic and copies ran while one was open for 9% -> 9% of each run, Pallas kernels for 0% -> 0%
where the time goes in v1:
time: 468 us; the launch traced here: 460 us
  waiting for transfers between devices  211 us (45%)
  local copies, waits for them, and re-layouts  125 us (27%)
  blocking collectives  48.1 us (10%)
  starting transfers between devices  35.4 us (8%)
  matrix products  14.2 us (3%)
  between operations  14 us (3%)
  other arithmetic  11.7 us (2%)
    all_to_all x1, waiting for transfers between devices, on_device(): own = lax.all_to_all(pick, 'dp', split_axis=0, concat_axis=0, tiled=True)  75.9 us
    all_to_all x1, waiting for transfers between devices, on_device(): lax.all_to_all(stacked, 'tensor', split_axis=2, concat_axis=0, tiled=True)  61.2 us
    all_to_all x1, blocking collectives, review_stocks(): lax.all_to_all(jnp.stack(pieces_in, 0), chip_axis, 0, 0)  48.1 us
    reduce_scatter x1, waiting for transfers between devices, on_device(): lax.psum_scatter(both, 'tensor', scatter_dimension=0, tiled=True)  44.1 us
    gather x1, local copies, waits for them, and re-layouts, on_device(): pick = with_zero_row(rows)[unit_list]  33.3 us
    unnamed x13, local copies, waits for them, and re-layouts  25.7 us
    all_to_all x1, waiting for transfers between devices, on_device(): lax.all_to_all(expert_out, 'dp', split_axis=0, concat_axis=0, tiled=True)  19.7 us
    slice x1, local copies, waits for them, and re-layouts, on_device(): own[:, 2, :]  18.2 us
  transfers between devices with their start and end apart: 5, of which 5 were waited for; matrix products, arithmetic and copies ran while one was open for 9% of the time, Pallas kernels for 0%

profile of v1, /device:TPU:1, one launch (start us, length us, event | category | flops | bytes accessed | tf_op | source)
XLA Modules:
  0.0 459.6 jit_solution(9944551154538953342)
XLA Ops:
  6.5 2.1 pad_maximum_fusion.1
  8.6 8.4 %copy.72 = bf16[56,3,8192]{0,1,2:T(4,128)(2,1)} copy(bf16[56,3,8192]{2,0,1:T(8,128)(2,1)S(1)} %pad_maximum_fusion.1) | data formatting | bytes 5505024 | tf_op jit(solution)/shard_map/stack | solution.py:44
  17.0 12.4 %reshape.163 = bf16[8,2,86016]{2,1,0:T(2,128)(2,1)} reshape(bf16[8192,3,56]{2,1,0:T(4,128)(2,1)} %bitcast.88) | data formatting | bytes 5505024
  29.4 9.1 %all-to-all-start.1 = ((bf16[8,2,86016]{2,1,0:T(2,128)(2,1)}), bf16[8,2,86016]{2,1,0:T(2,128)(2,1)S(1)}, u32[]{:S(2)}, u32[]{:S(2)}) async-start(bf16[8,2,86016]{2,1,0:T(2,128)(2,1)} %reshape.163), calls=%async_computation.1 | async-start | bytes 5505024 | tf_op jit(solution)/shard_map/all_to_all | solution.py:45
  38.6 1.2 reduce-window.16
  39.7 0.2 slice_reduce_fusion
  40.2 2.9 scatter_custom_fusion.1
  43.1 61.2 %all-to-all-done.1 = bf16[8,2,86016]{2,1,0:T(2,128)(2,1)S(1)} async-done(((bf16[8,2,86016]{2,1,0:T(2,128)(2,1)}), bf16[8,2,86016]{2,1,0:T(2,128)(2,1)S(1)}, u32[]{:S(2)}, u32[]{:S(2)}) %all-to-all-start.1) | async-done | bytes 2752544 | tf_op jit(solution)/shard_map/all_to_all | solution.py:45
  104.3 13.2 %reshape.164 = bf16[8192,3,56]{2,1,0:T(4,128)(2,1)} reshape(bf16[8,2,86016]{2,1,0:T(2,128)(2,1)S(1)} %all-to-all-done.1) | data formatting | bytes 5505024
  117.5 10.6 %copy.79 = bf16[56,3,8,1024]{3,0,2,1:T(8,128)(2,1)S(1)} copy(bf16[56,3,8,1024]{0,1,3,2:T(4,128)(2,1)} %bitcast.89) | data formatting | bytes 5505024 | tf_op jit(solution)/shard_map/all_to_all | solution.py:45
  128.1 2.4 copy.75
  130.5 3.2 concatenate.7
  133.7 33.3 %gather_fusion.1 = bf16[896,3,1024]{2,1,0:T(4,128)(2,1)} fusion(bf16[449,3,1024]{2,1,0:T(4,128)(2,1)} %concatenate.7, s32[1024]{0:T(1024)S(1)} %pad_clamp_fusion.1), kind=kCustom, calls=%fused_computation.1 | custom fusion | bytes 11013632 | tf_op jit(solution)/shard_map/gather | solution.py:48
  167.1 7.6 %all-to-all-start.2 = ((bf16[896,3,1024]{2,1,0:T(4,128)(2,1)}), bf16[896,3,1024]{2,1,0:T(4,128)(2,1)}, u32[]{:S(2)}, u32[]{:S(2)}) async-start(bf16[896,3,1024]{2,1,0:T(4,128)(2,1)} %gather_fusion.1), calls=%async_computation.2 | async-start | bytes 14680064 | tf_op jit(solution)/shard_map/all_to_all | solution.py:49
  174.7 0.1 copy.69
  174.9 0.1 eq.51
  175.0 0.1 eq.47
  175.2 1.1 constant_dynamic-slice_fusion
  176.3 1.2 reduce-window.14
  177.5 0.2 slice_reduce_fusion.1
  177.7 0.1 copy.68
  177.9 0.1 mul.52
  178.2 2.4 scatter_custom_fusion
  180.6 5.4 %gather_fusion = bf16[1024,1024]{1,0:T(8,128)(2,1)} fusion(bf16[257,1024]{1,0:T(8,128)(2,1)S(1)} %concatenate.6, s32[1024]{0:T(1024)S(1)} %fusion.21), kind=kCustom, calls=%fused_computation | custom fusion | bytes 4198400 | tf_op jit(solution)/shard_map/gather | solution.py:56
  186.0 75.9 %all-to-all-done.2 = bf16[896,3,1024]{2,1,0:T(4,128)(2,1)} async-done(((bf16[896,3,1024]{2,1,0:T(4,128)(2,1)}), bf16[896,3,1024]{2,1,0:T(4,128)(2,1)}, u32[]{:S(2)}, u32[]{:S(2)}) %all-to-all-start.2) | async-done | bytes 5505056 | tf_op jit(solution)/shard_map/all_to_all | solution.py:49
  261.9 8.7 %all-to-all-start = ((bf16[32,32,1024]{2,1,0:T(8,128)(2,1)}), bf16[32,32,1024]{2,1,0:T(8,128)(2,1)S(1)}, u32[]{:S(2)}, u32[]{:S(2)}) async-start(bf16[32,32,1024]{2,1,0:T(8,128)(2,1)} %bitcast.4), calls=%async_computation | async-start | bytes 4194304 | tf_op jit(solution)/shard_map/all_to_all | solution.py:57
  270.7 18.2 %fusion.28 = (bf16[896,1,1024]{2,1,0:T(2,128)(2,1)}, bf16[896,1,1024]{2,1,0:T(2,128)(2,1)}, bf16[896,1,1024]{2,1,0:T(2,128)(2,1)}) fusion(bf16[896,3,1024]{2,1,0:T(4,128)(2,1)} %all-to-all-done.2), kind=kLoop, calls=%fused_computation.70 | loop fusion | bytes 11010048 | tf_op jit(solution)/shard_map/slice | solution.py:64
  288.9 10.1 %all-to-all-done = bf16[32,32,1024]{2,1,0:T(8,128)(2,1)S(1)} async-done(((bf16[32,32,1024]{2,1,0:T(8,128)(2,1)}), bf16[32,32,1024]{2,1,0:T(8,128)(2,1)S(1)}, u32[]{:S(2)}, u32[]{:S(2)}) %all-to-all-start) | async-done | bytes 2097184 | tf_op jit(solution)/shard_map/all_to_all | solution.py:57
  298.9 4.6 convert_bitcast_fusion.1
  303.5 2.4 convert_bitcast_fusion
  305.9 2.2 pad_maximum_fusion
  308.1 44.1 %reduce-scatter.2.cloned.1.call-done = bf16[128,2,896]{2,0,1:T(8,128)(2,1)} async-done(((bf16[1024,2,896]{2,0,1:T(8,128)(2,1)}), bf16[128,2,896]{2,0,1:T(8,128)(2,1)}) %reduce-scatter.2.cloned.1.call-update) | async-done | bytes 458768 | tf_op jit(solution)/shard_map/reduce_scatter | solution.py:61
  352.2 1.1 convert_element_type.42
  353.2 0.1 fusion.13
  353.4 0.2 stack.39
  353.6 48.1 %all_to_all.52 = bf16[8,128,896]{2,1,0:T(8,128)(2,1)S(1)} all-to-all(bf16[8,128,896]{2,1,0:T(8,128)(2,1)S(1)} %stack.39), channel_id=1, replica_groups=mesh['dp'=32,'tensor'=8] {'tensor'}, dimensions={0} | all-to-all | bytes 3670016 | tf_op jit(solution)/shard_map/all_to_all | solution.py:11
  401.8 3.7 convolution_convert_fusion
  405.5 9.8 %all-to-all-start.4 = ((bf16[32,32,1024]{2,1,0:T(8,128)(2,1)}), bf16[32,32,1024]{2,1,0:T(8,128)(2,1)S(1)}, u32[]{:S(2)}, u32[]{:S(2)}) async-start(bf16[32,32,1024]{2,1,0:T(8,128)(2,1)} %bitcast.91), calls=%async_computation.5 | async-start | bytes 4194304 | tf_op jit(solution)/shard_map/all_to_all | solution.py:67
  415.3 0.1 copy.65
  415.5 0.1 reshape.128
  415.6 3.5 fusion.29
  419.2 4.5 gather_fusion.3
  423.7 0.1 reshape.131
  424.0 0.1 copy.67
  424.2 19.7 %all-to-all-done.4 = bf16[32,32,1024]{2,1,0:T(8,128)(2,1)S(1)} async-done(((bf16[32,32,1024]{2,1,0:T(8,128)(2,1)}), bf16[32,32,1024]{2,1,0:T(8,128)(2,1)S(1)}, u32[]{:S(2)}, u32[]{:S(2)}) %all-to-all-start.4) | async-done | bytes 2097184 | tf_op jit(solution)/shard_map/all_to_all | solution.py:67
  443.8 2.8 gather_fusion.2
  446.6 2.4 reshape.103
  449.0 3.5 multiply_reduce_fusion
  (36 shorter events, 0.6 us)
Async XLA Ops:
  6.5 409.1 %copy-start = (bf16[8192,32]{0,1:T(8,128)(2,1)S(1)}, bf16[8192,32]{0,1:T(8,128)(2,1)}, u32[]{:S(2)}) copy-start(bf16[8192,32]{0,1:T(8,128)(2,1)} %param.8) | copy-start | bytes 1572868
  29.4 9.1 %copy-start.4 = (s32[448,1]{0,1:T(1,128)S(1)}, s32[448,1]{0,1:T(1,128)}, u32[]{:S(2)}) copy-start(s32[448,1]{0,1:T(1,128)} %param.12) | copy-start | bytes 5380
  29.4 74.9 %all-to-all-start.1 = ((bf16[8,2,86016]{2,1,0:T(2,128)(2,1)}), bf16[8,2,86016]{2,1,0:T(2,128)(2,1)S(1)}, u32[]{:S(2)}, u32[]{:S(2)}) async-start(bf16[8,2,86016]{2,1,0:T(2,128)(2,1)} %reshape.163), calls=%async_computation.1 | async-start | bytes 5505024 | tf_op jit(solution)/shard_map/all_to_all | solution.py:45
  167.1 7.7 %copy-start.3 = (s32[256,2]{0,1:T(2,128)S(1)}, s32[256,2]{0,1:T(2,128)}, u32[]{:S(2)}) copy-start(s32[256,2]{0,1:T(2,128)} %param.13) | copy-start | bytes 6148
  167.1 94.8 %all-to-all-start.2 = ((bf16[896,3,1024]{2,1,0:T(4,128)(2,1)}), bf16[896,3,1024]{2,1,0:T(4,128)(2,1)}, u32[]{:S(2)}, u32[]{:S(2)}) async-start(bf16[896,3,1024]{2,1,0:T(4,128)(2,1)} %gather_fusion.1), calls=%async_computation.2 | async-start | bytes 14680064 | tf_op jit(solution)/shard_map/all_to_all | solution.py:49
  261.9 37.0 %all-to-all-start = ((bf16[32,32,1024]{2,1,0:T(8,128)(2,1)}), bf16[32,32,1024]{2,1,0:T(8,128)(2,1)S(1)}, u32[]{:S(2)}, u32[]{:S(2)}) async-start(bf16[32,32,1024]{2,1,0:T(8,128)(2,1)} %bitcast.4), calls=%async_computation | async-start | bytes 4194304 | tf_op jit(solution)/shard_map/all_to_all | solution.py:57
  270.6 81.5 %reduce-scatter.2.cloned.1.call-start = ((), (), s32[]{:S(2)}) async-start(), calls=%async_computation.6 | async-start | bytes 4128768 | tf_op jit(solution)/shard_map/reduce_scatter | solution.py:61
  298.9 4.6 copy-start.2
  353.4 48.4 %copy-start.1 = (bf16[896,1,1024]{2,1,0:T(2,128)(2,1)S(1)}, bf16[896,1,1024]{2,1,0:T(2,128)(2,1)}, u32[]{:S(2)}) copy-start(bf16[896,1,1024]{2,1,0:T(2,128)(2,1)} %get-tuple-element.7) | copy-start | bytes 5505028
  405.5 38.3 %all-to-all-start.4 = ((bf16[32,32,1024]{2,1,0:T(8,128)(2,1)}), bf16[32,32,1024]{2,1,0:T(8,128)(2,1)S(1)}, u32[]{:S(2)}, u32[]{:S(2)}) async-start(bf16[32,32,1024]{2,1,0:T(8,128)(2,1)} %bitcast.91), calls=%async_computation.5 | async-start | bytes 4194304 | tf_op jit(solution)/shard_map/all_to_all | solution.py:67
Sparse Core Ops, SparseCore 0:
  308.2 43.9 reduce-scatter.1
